TPU v7x, 256 devices: a whole 4x4x8 slice. The times are simulated.
256 devices in a mesh: seq: 64 (over x, z, core), ch: 4 (over y).
Axes of the slice: x: 4, y: 4, z: 8, core: 2. Of those that a mesh axis runs over, the one named last changes fastest.
Arguments:
- inputs: bfloat16 [8192, 4096], P('seq'), may hold values from -6 to 6
- norm_gain: float32 [4096], replicated, may hold values from 0.1 to 1.9
- in_weight: bfloat16 [4096, 3, 1024], P('seq', None, 'ch'), may hold values from -0.09375 to 0.09375
- short_filter: float32 [3, 3, 1024], P(None, None, 'ch'), may hold values from -4 to 4
- long_filter: float32 [8192, 1024], P('seq', 'ch'), may hold values from -2.2 to 2.2
- conv_bias: float32 [1024], P('ch'), may hold values from -4 to 4
- out_weight: bfloat16 [1024, 4096], P('ch', 'seq'), may hold values from -0.1875 to 0.1875
- out_grad: bfloat16 [8192, 4096], P('seq'), may hold values from -6 to 6
Outputs:
- block_out: bfloat16 [8192, 4096], P('seq', 'ch')
- in_grad: bfloat16 [8192, 4096], P('seq')
- filter_grad: float32 [8192, 1024], P('seq', 'ch')
All inputs are finite; a program needn't handle non-finite values.
Results may differ from a plain program's by a relative error of at most 0.013.
Values may be sent and summed in bfloat16 or wider, within the bound.
No kernel may reach another device: no remote copies, remote signals or barrier semaphores. Data moves between devices by JAX's collectives and lax.ppermute only.
A program may use at most 64 MiB of HBM per device.

v0:
```python
import math
import jax
import jax.numpy as jnp
from jax import lax
from jax.sharding import PartitionSpec as P

epsilon = 1e-05
highest = lax.Precision.HIGHEST


def passed_along(block, axis, distance):
    devices = range(lax.axis_size(axis))
    route = [(i - distance, i) for i in devices if i - distance in devices]
    return lax.ppermute(block, axis, route)


def to_columns(signals):
    return lax.all_to_all(signals, "seq", split_axis=1, concat_axis=2, tiled=True)


def to_rows(signals):
    return lax.all_to_all(signals, "seq", split_axis=2, concat_axis=1, tiled=True)


def turn_table(rows, cols, period, sign):
    turns = jnp.arange(rows, dtype=jnp.int32)[:, None] * jnp.arange(cols, dtype=jnp.int32)[None, :]
    phases = sign * 2.0 * math.pi / period * (turns % period).astype(jnp.float32)
    return (jnp.cos(phases), jnp.sin(phases))


def fft_sizes(seq_total):
    total = 2 * seq_total
    inner = 1
    while inner * inner < total:
        inner *= 2
    return (total // inner, inner)


def forward_dft(signals):
    count, chans, seq_total = signals.shape
    outer, inner = fft_sizes(seq_total)
    grid = signals.reshape(count, chans, outer // 2, inner)
    cos_out, sin_out = turn_table(outer, outer // 2, outer, 1.0)
    first_real = jnp.einsum("kn,ucnm->uckm", cos_out, grid, precision=highest)
    first_imag = -jnp.einsum("kn,ucnm->uckm", sin_out, grid, precision=highest)
    cos_tw, sin_tw = turn_table(outer, inner, outer * inner, 1.0)
    turned_real = first_real * cos_tw + first_imag * sin_tw
    turned_imag = first_imag * cos_tw - first_real * sin_tw
    cos_in, sin_in = turn_table(inner, inner, inner, 1.0)
    spec_real = jnp.einsum("uckm,mj->uckj", turned_real, cos_in, precision=highest) + jnp.einsum(
        "uckm,mj->uckj", turned_imag, sin_in, precision=highest
    )
    spec_imag = jnp.einsum("uckm,mj->uckj", turned_imag, cos_in, precision=highest) - jnp.einsum(
        "uckm,mj->uckj", turned_real, sin_in, precision=highest
    )
    return (spec_real, spec_imag)


def inverse_dft(spec_real, spec_imag):
    count, chans, outer, inner = spec_real.shape
    cos_in, sin_in = turn_table(inner, inner, inner, 1.0)
    back_real = jnp.einsum("uckj,jm->uckm", spec_real, cos_in, precision=highest) - jnp.einsum(
        "uckj,jm->uckm", spec_imag, sin_in, precision=highest
    )
    back_imag = jnp.einsum("uckj,jm->uckm", spec_imag, cos_in, precision=highest) + jnp.einsum(
        "uckj,jm->uckm", spec_real, sin_in, precision=highest
    )
    cos_tw, sin_tw = turn_table(outer, inner, outer * inner, 1.0)
    turned_real = back_real * cos_tw - back_imag * sin_tw
    turned_imag = back_imag * cos_tw + back_real * sin_tw
    cos_out, sin_out = turn_table(outer, outer // 2, outer, 1.0)
    grid = jnp.einsum("kn,uckm->ucnm", cos_out, turned_real, precision=highest) - jnp.einsum(
        "kn,uckm->ucnm", sin_out, turned_imag, precision=highest
    )
    return grid.reshape(count, chans, outer * inner // 2) / float(outer * inner)


def per_device(
    inputs, norm_gain, in_weight, short_filter, long_filter, conv_bias, out_weight, out_grad
):
    local_rows = inputs.shape[0]
    model_width = inputs.shape[1]
    slab_width = long_filter.shape[1]
    taps = short_filter.shape[1]
    wide_inputs = inputs.astype(jnp.float32)
    inv_rms = lax.rsqrt(jnp.mean(wide_inputs * wide_inputs, axis=1, keepdims=True) + epsilon)
    normed = (wide_inputs * inv_rms * norm_gain).astype(jnp.bfloat16)
    in_panel, out_panel = (
        lax.all_gather(in_weight, "seq", axis=0, tiled=True),
        lax.all_gather(out_weight, "seq", axis=1, tiled=True),
    )
    in_flat = in_panel.reshape(model_width, 3 * slab_width)
    projected = jnp.dot(normed, in_flat, preferred_element_type=jnp.float32)
    projected = projected.astype(jnp.bfloat16).reshape(local_rows, 3, slab_width)
    upper_rim = passed_along(projected[local_rows - (taps - 1) :], "seq", 1)
    extended = jnp.concatenate([upper_rim, projected], 0).astype(jnp.float32)
    mixed = jnp.zeros((local_rows, 3, slab_width), jnp.float32)
    for offset in range(taps):
        begin = taps - 1 - offset
        mixed = mixed + short_filter[:, offset, :][None] * extended[begin : begin + local_rows]
    query_br = mixed[:, 0]
    key_br = mixed[:, 1]
    value_br = mixed[:, 2]
    product = key_br * value_br
    gate_grad = jnp.dot(out_grad, out_panel.T, preferred_element_type=jnp.float32)
    carried = gate_grad * query_br
    columns = to_columns(jnp.stack([product, long_filter, carried]).transpose(0, 2, 1))
    all_real, all_imag = forward_dft(columns)
    sig_real, filt_real, grad_real = (all_real[0], all_real[1], all_real[2])
    sig_imag, filt_imag, grad_imag = (all_imag[0], all_imag[1], all_imag[2])
    conv_real = sig_real * filt_real - sig_imag * filt_imag
    conv_imag = sig_real * filt_imag + sig_imag * filt_real
    back_real = grad_real * filt_real + grad_imag * filt_imag
    back_imag = grad_imag * filt_real - grad_real * filt_imag
    pair_real = grad_real * sig_real + grad_imag * sig_imag
    pair_imag = grad_imag * sig_real - grad_real * sig_imag
    outs = inverse_dft(
        jnp.stack([conv_real, back_real, pair_real]), jnp.stack([conv_imag, back_imag, pair_imag])
    )
    returned = to_rows(outs).transpose(0, 2, 1)
    conv_out = returned[0]
    back_conv = returned[1]
    filter_grad = returned[2] * float(local_rows * lax.axis_size("seq")) ** (-0.5)
    biased = conv_out + conv_bias * product
    gated = (query_br * biased).astype(jnp.bfloat16)
    partial_out = jnp.dot(gated, out_panel, preferred_element_type=jnp.float32)
    summed = lax.psum_scatter(
        partial_out.astype(jnp.bfloat16), "ch", scatter_dimension=1, tiled=True
    ).astype(jnp.float32)
    share = summed.shape[1]
    residual = lax.dynamic_slice_in_dim(wide_inputs, lax.axis_index("ch") * share, share, 1)
    block_out = (residual + summed).astype(jnp.bfloat16)
    source_grad = back_conv + conv_bias * carried
    mixed_grad = jnp.stack([gate_grad * biased, source_grad * value_br, source_grad * key_br], 1)
    lower_rim = passed_along(mixed_grad[: taps - 1], "seq", -1)
    extended_back = jnp.concatenate([mixed_grad, lower_rim], 0)
    proj_grad = jnp.zeros((local_rows, 3, slab_width), jnp.float32)
    for offset in range(taps):
        proj_grad = (
            proj_grad
            + short_filter[:, offset, :][None] * extended_back[offset : offset + local_rows]
        )
    proj_grad = proj_grad.astype(jnp.bfloat16).reshape(local_rows, 3 * slab_width)
    partial_grad = jnp.dot(proj_grad, in_flat.T, preferred_element_type=jnp.float32)
    norm_grad = lax.psum(partial_grad, "ch")
    weighted = norm_grad * norm_gain
    inner_term = jnp.mean(weighted * wide_inputs, axis=1, keepdims=True)
    in_grad = (
        out_grad.astype(jnp.float32) + weighted * inv_rms - wide_inputs * inv_rms**3 * inner_term
    ).astype(jnp.bfloat16)
    return (block_out, in_grad, filter_grad)


def solution(mesh):
    return jax.shard_map(
        per_device,
        mesh=mesh,
        in_specs=(
            P("seq", None),
            P(),
            P("seq", None, "ch"),
            P(None, None, "ch"),
            P("seq", "ch"),
            P("ch"),
            P("ch", "seq"),
            P("seq", None),
        ),
        out_specs=(P("seq", "ch"), P("seq", None), P("seq", "ch")),
        check_vma=False,
    )
```

profile of v0, /device:TPU:1, one launch (start us, length us, event | category | flops | bytes accessed | tf_op | source)
XLA Modules:
  0.0 393.4 jit_solution(6677568835043596494)
XLA Ops:
  7.2 0.7 all-gather.3.cloned.1.call-update
  7.9 0.7 all-gather.5.cloned.1.call-update
  8.6 0.8 fusion.142
  9.5 1.5 multiply_reduce_fusion.1
  11.0 0.6 multiply_multiply_fusion
  11.6 83.9 %all-gather.3.cloned.1.call-done = bf16[4096,3,256]{2,0,1:T(8,128)(2,1)} async-done(((bf16[64,3,256]{2,0,1:T(8,128)(2,1)}), bf16[4096,3,256]{2,0,1:T(8,128)(2,1)}) %all-gather.3.cloned.1.call-update) | async-done | bytes 6291472 | tf_op jit(solution)/shard_map/all_gather | solution.py:89
  95.5 8.7 %copy.46 = bf16[4096,3,256]{0,2,1:T(8,128)(2,1)} copy(bf16[4096,3,256]{2,0,1:T(8,128)(2,1)} %all-gather.3.cloned.1.call-done) | data formatting | bytes 12582912 | tf_op jit(solution)/shard_map/all_gather | solution.py:89
  104.2 5.1 %convolution_convert_fusion.1 = bf16[128,768]{1,0:T(8,128)(2,1)S(1)} fusion(bf16[4096,768]{0,1:T(8,128)(2,1)} %bitcast.127, bf16[128,4096]{1,0:T(8,128)(2,1)S(1)} %copy-done, f32[4096]{0:T(1024)S(1)} %copy-done.9, f32[128]{0:T(128)S(1)} %get-tuple-element.19), kind=kOutput, calls=%fused_computation.16 | convolution fusion | flops 807501824 | bytes 7553536 | tf_op jit(solution)/shard_map/dot_general | solution.py:93
  109.3 2.7 collective-permute-start
  112.1 60.2 %all-gather.5.cloned.1.call-done = bf16[256,4096]{0,1:T(8,128)(2,1)} async-done(((bf16[256,64]{0,1:T(8,128)(2,1)}), bf16[256,4096]{0,1:T(8,128)(2,1)}) %all-gather.5.cloned.1.call-update) | async-done | bytes 2097168 | tf_op jit(solution)/shard_map/all_gather | solution.py:90
  172.3 2.0 fusion.143
  175.4 1.0 copy.50
  176.4 6.6 %all-to-all-start = ((f32[3,256,128]{2,0,1:T(4,128)}), f32[3,256,128]{2,0,1:T(4,128)S(1)}, u32[]{:S(2)}, u32[]{:S(2)}) async-start(f32[3,256,128]{2,0,1:T(4,128)} %copy.50), calls=%async_computation | async-start | bytes 1048576 | tf_op jit(solution)/shard_map/all_to_all | solution.py:18
  183.9 16.3 %all-to-all-done = f32[3,256,128]{2,0,1:T(4,128)S(1)} async-done(((f32[3,256,128]{2,0,1:T(4,128)}), f32[3,256,128]{2,0,1:T(4,128)S(1)}, u32[]{:S(2)}, u32[]{:S(2)}) %all-to-all-start) | async-done | bytes 393248 | tf_op jit(solution)/shard_map/all_to_all | solution.py:18
  200.3 1.5 convolution_bitcast_fusion.1
  201.8 1.5 fusion
  203.3 1.6 fusion.31
  204.9 1.6 fusion.32
  206.5 1.6 convolution_add_fusion.1
  208.1 1.6 convolution_subtract_fusion.1
  209.9 1.1 fusion.13
  211.0 1.3 fusion.12
  212.4 1.1 convolution_subtract_fusion
  213.5 1.1 convolution_add_fusion
  214.6 1.2 fusion.8
  215.8 1.2 fusion.2
  217.0 8.6 %copy.85 = f32[3,4,64,128]{1,0,3,2:T(4,128)} copy(f32[3,4,64,128]{3,2,1,0:T(8,128)S(1)} %fusion.2) | data formatting | bytes 786432 | tf_op jit(solution)/shard_map/div | solution.py:75
  225.6 16.0 %reshape.105 = f32[64,1,1536]{2,1,0:T(1,128)S(1)} reshape(f32[8192,3,4]{2,1,0:T(4,128)} %bitcast.125) | data formatting | bytes 786432
  241.6 20.6 %all_to_all.33 = f32[64,1,1536]{2,1,0:T(1,128)S(1)} all-to-all(f32[64,1,1536]{2,1,0:T(1,128)S(1)} %reshape.105), channel_id=1, replica_groups=mesh['seq'=64,'ch'=4] {'seq'}, dimensions={0} | all-to-all | bytes 786432 | tf_op jit(solution)/shard_map/all_to_all | solution.py:22
  262.8 1.6 reduce
  264.4 11.6 %reshape.106 = f32[8192,3,4]{2,1,0:T(4,128)} reshape(f32[64,1536]{1,0:T(8,128)S(1)} %reduce) | data formatting | bytes 786432
  275.9 10.1 %copy.86 = f32[3,4,64,128]{3,2,1,0:T(8,128)} copy(f32[3,4,64,128]{1,0,3,2:T(4,128)} %bitcast.126) | data formatting | bytes 786432 | tf_op jit(solution)/shard_map/all_to_all | solution.py:22
  286.0 2.2 copy.67
  288.1 1.9 copy.68
  290.0 1.8 fusion.37
  291.9 1.8 convolution_convert_fusion
  293.7 1.0 fusion.38
  294.7 1.0 pad_maximum_fusion.7
  295.7 2.6 collective-permute-start.1
  298.3 2.4 collective-permute-done.1
  300.7 6.4 %convolution_bitcast_fusion = f32[128,4096]{1,0:T(8,128)} fusion(bf16[4096,3,256]{2,0,1:T(8,128)(2,1)} %all-gather.3.cloned.1.call-done, f32[130,3,256]{2,0,1:T(8,128)S(1)} %pad_maximum_fusion.6, f32[3,256]{1,0:T(4,128)S(1)} %get-tuple-element.20, f32[3,256]{1,0:T(4,128)S(1)} %get-tuple-element.21, f32[3,256]{1,0:T(4,128)S(1)} %bitcast.136, ...), kind=kOutput, calls=%fused_computation | convolution fusion | flops 806092800 | bytes 9580544 | tf_op jit(solution)/shard_map/dot_general | solution.py:144
  307.2 1.6 convert_element_type.86
  308.7 1.6 fusion.33
  310.3 5.3 %reduce-scatter.2.cloned.1.call-done = bf16[128,1024]{1,0:T(8,128)(2,1)} async-done(((bf16[128,4096]{1,0:T(8,128)(2,1)}), bf16[128,1024]{1,0:T(8,128)(2,1)}) %reduce-scatter.2.cloned.1.call-update) | async-done | bytes 262160 | tf_op jit(solution)/shard_map/reduce_scatter | solution.py:127
  315.6 1.9 add_convert_fusion
  317.5 65.3 %all-reduce.2.cloned.1.call-done = f32[128,4096]{1,0:T(8,128)} async-done(((f32[128,4096]{1,0:T(8,128)}), f32[128,4096]{1,0:T(8,128)}) %all-reduce.2.cloned.1.call-update) | async-done | bytes 2097168 | tf_op jit(solution)/shard_map/psum | solution.py:145
  382.8 2.1 multiply_reduce_fusion
  385.0 1.9 subtract_convert_fusion
  (57 shorter events, 2.9 us)
Async XLA Ops:
  7.2 88.3 %all-gather.3.cloned.1.call-start = ((), (), s32[]{:S(2)}) async-start(), calls=%async_computation.3 | async-start | bytes 6389760 | tf_op jit(solution)/shard_map/all_gather | solution.py:89
  7.9 164.4 %all-gather.5.cloned.1.call-start = ((), (), s32[]{:S(2)}) async-start(), calls=%async_computation.4 | async-start | bytes 2129920 | tf_op jit(solution)/shard_map/all_gather | solution.py:90
  11.6 92.6 %copy-start.13 = (f32[128]{0:T(128)}, f32[128]{0:T(128)S(1)}, u32[]{:S(2)}) copy-start(f32[128]{0:T(128)S(1)} %get-tuple-element.19) | copy-start | bytes 1540
  11.6 92.6 %copy-start = (bf16[128,4096]{1,0:T(8,128)(2,1)S(1)}, bf16[128,4096]{1,0:T(8,128)(2,1)}, u32[]{:S(2)}) copy-start(bf16[128,4096]{1,0:T(8,128)(2,1)} %param.8) | copy-start | bytes 3145732
  11.6 92.6 %copy-start.9 = (f32[4096]{0:T(1024)S(1)}, f32[4096]{0:T(1024)}, u32[]{:S(2)}) copy-start(f32[4096]{0:T(1024)} %param.9) | copy-start | bytes 49156
  104.2 68.1 %copy-start.3 = (bf16[128,4096]{1,0:T(8,128)(2,1)S(1)}, bf16[128,4096]{1,0:T(8,128)(2,1)}, u32[]{:S(2)}) copy-start(bf16[128,4096]{1,0:T(8,128)(2,1)} %param.15) | copy-start | bytes 3145732
  109.3 65.4 %collective-permute-start = (bf16[2,3,256]{2,0,1:T(2,128)(2,1)S(1)}, bf16[2,3,256]{2,0,1:T(2,128)(2,1)S(1)}, u32[]{:S(2)}, u32[]{:S(2)}) collective-permute-start(bf16[2,3,256]{2,0,1:T(2,128)(2,1)S(1)} %bitcast.138), channel_id=1, source_target_pairs={{0,4},{4,8},{8,12},{12,16},{16,20},{20,24},{24,28},{28,32},{32,36}... | collective-permute-start | bytes 9224 | tf_op jit(solution)/shard_map/ppermute | solution.py:14
  174.4 1.0 copy-start.7
  174.4 1.0 copy-start.8
  176.4 23.9 %all-to-all-start = ((f32[3,256,128]{2,0,1:T(4,128)}), f32[3,256,128]{2,0,1:T(4,128)S(1)}, u32[]{:S(2)}, u32[]{:S(2)}) async-start(f32[3,256,128]{2,0,1:T(4,128)} %copy.50), calls=%async_computation | async-start | bytes 1048576 | tf_op jit(solution)/shard_map/all_to_all | solution.py:18
  183.0 132.6 %reduce-scatter.2.cloned.1.call-start = ((), (), s32[]{:S(2)}) async-start(), calls=%async_computation.5 | async-start | bytes 1310720 | tf_op jit(solution)/shard_map/reduce_scatter | solution.py:127
  275.9 14.1 %copy-start.11 = (f32[256]{0:T(256)S(1)}, f32[256]{0:T(256)}, u32[]{:S(2)}) copy-start(f32[256]{0:T(256)} %param.13) | copy-start | bytes 3076
  286.0 5.9 %copy-start.1 = (bf16[256,4096]{0,1:T(8,128)(2,1)S(1)}, bf16[256,4096]{0,1:T(8,128)(2,1)}, u32[]{:S(2)}) copy-start(bf16[256,4096]{0,1:T(8,128)(2,1)} %all-gather.5.cloned.1.call-done) | copy-start | bytes 6291460
  293.6 7.0 %copy-start.5 = (f32[128,1,256]{2,0,1:T(8,128)S(1)}, f32[128,1,256]{2,0,1:T(8,128)}, u32[]{:S(2)}) copy-start(f32[128,1,256]{2,0,1:T(8,128)} %get-tuple-element.5) | copy-start | bytes 393220
  293.6 7.0 %copy-start.6 = (f32[128,1,256]{2,0,1:T(8,128)S(1)}, f32[128,1,256]{2,0,1:T(8,128)}, u32[]{:S(2)}) copy-start(f32[128,1,256]{2,0,1:T(8,128)} %get-tuple-element.13) | copy-start | bytes 393220
  293.7 89.1 %all-reduce.2.cloned.1.call-start = ((), (), s32[]{:S(2)}) async-start(), calls=%async_computation.6 | async-start | bytes 4194304 | tf_op jit(solution)/shard_map/psum | solution.py:145
  295.7 4.9 %collective-permute-start.1 = (f32[2,3,256]{2,0,1:T(2,128)S(1)}, f32[2,3,256]{2,0,1:T(2,128)S(1)}, u32[]{:S(2)}, u32[]{:S(2)}) collective-permute-start(f32[2,3,256]{2,0,1:T(2,128)S(1)} %slice.110), channel_id=1, source_target_pairs={{4,0},{8,4},{12,8},{16,12},{20,16},{24,20},{28,24},{32,28},{36,32}... | collective-permute-start | bytes 18440 | tf_op jit(solution)/shard_map/ppermute | solution.py:14
  307.1 75.6 %copy-start.10 = (f32[4096]{0:T(1024)S(1)}, f32[4096]{0:T(1024)}, u32[]{:S(2)}) copy-start(f32[4096]{0:T(1024)} %param.9) | copy-start | bytes 49156
  310.3 74.6 %copy-start.4 = (bf16[128,4096]{1,0:T(8,128)(2,1)S(1)}, bf16[128,4096]{1,0:T(8,128)(2,1)}, u32[]{:S(2)}) copy-start(bf16[128,4096]{1,0:T(8,128)(2,1)} %param.15) | copy-start | bytes 3145732
  310.3 74.6 %copy-start.12 = (f32[128]{0:T(128)S(1)}, f32[128]{0:T(128)}, u32[]{:S(2)}) copy-start(f32[128]{0:T(128)} %get-tuple-element.18) | copy-start | bytes 1540
  310.3 74.6 %copy-start.14 = (f32[128]{0:T(128)S(1)}, f32[128]{0:T(128)}, u32[]{:S(2)}) copy-start(f32[128]{0:T(128)} %copy-done.13) | copy-start | bytes 1540
  382.8 2.2 copy-start.2
Sparse Core Ops, SparseCore 0:
  10.8 84.6 all-gather.2
  98.3 74.0 all-gather.4
  293.8 21.7 reduce-scatter.1
  317.8 64.9 all-reduce.1
where the time goes:
time: 395 us; the launch traced here: 393 us
  waiting for transfers between devices  235 us (59%)
  local copies, waits for them, and re-layouts  62.4 us (16%)
  matrix products  31.7 us (8%)
  blocking collectives  20.6 us (5%)
  other arithmetic  17.5 us (4%)
  between operations  14.1 us (4%)
  starting transfers between devices  12.2 us (3%)
    all_gather x1, waiting for transfers between devices, per_device(): lax.all_gather(in_weight, 'seq', axis=0, tiled=True)  83.9 us
    psum x1, waiting for transfers between devices, per_device(): norm_grad = lax.psum(partial_grad, 'ch')  65.3 us
    all_gather x1, waiting for transfers between devices, per_device(): lax.all_gather(out_weight, 'seq', axis=1, tiled=True)  60.2 us
    unnamed x34, local copies, waits for them, and re-layouts  28.1 us
    all_to_all x1, blocking collectives, to_rows(): lax.all_to_all(signals, 'seq', split_axis=2, concat_axis=1, tiled=True)  20.6 us
    all_to_all x1, waiting for transfers between devices, to_columns(): lax.all_to_all(signals, 'seq', split_axis=1, concat_axis=2, tiled=True)  16.3 us
    all_to_all x4, local copies, waits for them, and re-layouts, to_rows(): lax.all_to_all(signals, 'seq', split_axis=2, concat_axis=1, tiled=True)  14.6 us
    all_gather x1, local copies, waits for them, and re-layouts, per_device(): lax.all_gather(in_weight, 'seq', axis=0, tiled=True)  8.7 us
  transfers between devices with their start and end apart: 7, of which 6 were waited for; matrix products, arithmetic and copies ran while one was open for 8% of the time, Pallas kernels for 0%

commit v1 on v0

--- a/solution.py
+++ b/solution.py
@@ -87,7 +87,12 @@
     normed = (wide_inputs * inv_rms * norm_gain).astype(jnp.bfloat16)
     in_panel, out_panel = (
         lax.all_gather(in_weight, "seq", axis=0, tiled=True),
-        lax.all_gather(out_weight, "seq", axis=1, tiled=True),
+        jnp.concatenate(
+            lax.all_to_all(
+                jnp.stack([out_weight for _ in range(lax.axis_size("seq"))]), "seq", 0, 0
+            ),
+            axis=1,
+        ),
     )
     in_flat = in_panel.reshape(model_width, 3 * slab_width)
     projected = jnp.dot(normed, in_flat, preferred_element_type=jnp.float32)

time: 395 us -> 353 us (0.89)
  waiting for transfers between devices: 235 us -> 165 us
  starting transfers between devices: 12.2 us -> 27.5 us
  local copies, waits for them, and re-layouts: 62.4 us -> 71.1 us
    all_gather x1 -> x0, waiting for transfers between devices: 60.2 us -> none  [per_device(): lax.all_gather(out_weight, 'seq', axis=1, tiled=True)]
    all_to_all x0 -> x1, starting transfers between devices: none -> 13.1 us  [per_device(): lax.all_to_all(jnp.stack([out_weight for _ in range(lax.axis_size('seq'))...]
    all_gather x1, waiting for transfers between devices: 83.9 us -> 76.3 us  [per_device(): lax.all_gather(in_weight, 'seq', axis=0, tiled=True)]
    all_to_all x1, waiting for transfers between devices: 16.3 us -> 12.1 us  [to_columns(): lax.all_to_all(signals, 'seq', split_axis=1, concat_axis=2, tiled=True)]
    unnamed x34 -> x30, local copies, waits for them, and re-layouts: 28.1 us -> 29.9 us
  transfers between devices with their start and end apart: 7 -> 7, of which waited for: 6 -> 5; matrix products, arithmetic and copies ran while one was open for 8% -> 10% of each run, Pallas kernels for 0% -> 0%
where the time goes in v1:
time: 353 us; the launch traced here: 351 us
  waiting for transfers between devices  165 us (47%)
  local copies, waits for them, and re-layouts  71.1 us (20%)
  matrix products  35.6 us (10%)
  starting transfers between devices  27.5 us (8%)
  blocking collectives  20.9 us (6%)
  other arithmetic  17 us (5%)
  between operations  14.1 us (4%)
    all_gather x1, waiting for transfers between devices, per_device(): lax.all_gather(in_weight, 'seq', axis=0, tiled=True)  76.3 us
    psum x1, waiting for transfers between devices, per_device(): norm_grad = lax.psum(partial_grad, 'ch')  65.5 us
    unnamed x30, local copies, waits for them, and re-layouts  29.9 us
    all_to_all x1, blocking collectives, to_rows(): lax.all_to_all(signals, 'seq', split_axis=2, concat_axis=1, tiled=True)  20.9 us
    all_to_all x4, local copies, waits for them, and re-layouts, to_rows(): lax.all_to_all(signals, 'seq', split_axis=2, concat_axis=1, tiled=True)  14.5 us
    all_to_all x1, starting transfers between devices, per_device(): lax.all_to_all(jnp.stack([out_weight for _ in range(lax.axis_size('seq'))...  13.1 us
    all_to_all x1, waiting for transfers between devices, to_columns(): lax.all_to_all(signals, 'seq', split_axis=1, concat_axis=2, tiled=True)  12.1 us
    div x1, local copies, waits for them, and re-layouts, inverse_dft(): return grid.reshape(count, chans, outer * inner // 2) / float(outer * inner)  9.6 us
  transfers between devices with their start and end apart: 7, of which 5 were waited for; matrix products, arithmetic and copies ran while one was open for 10% of the time, Pallas kernels for 0%

profile of v1, /device:TPU:1, one launch (start us, length us, event | category | flops | bytes accessed | tf_op | source)
XLA Modules:
  0.0 350.8 jit_solution(16134197943182970012)
XLA Ops:
  7.2 0.7 all-gather.2.cloned.1.call-update
  7.9 2.4 stack.21
  10.3 13.1 %all-to-all-start = ((bf16[64,256,64]{1,2,0:T(8,128)(2,1)}), bf16[64,256,64]{1,2,0:T(8,128)(2,1)S(1)}, u32[]{:S(2)}, u32[]{:S(2)}) async-start(bf16[64,256,64]{1,2,0:T(8,128)(2,1)} %stack.21), calls=%async_computation | async-start | bytes 4194304 | tf_op jit(solution)/shard_map/all_to_all | solution.py:91
  24.3 76.3 %all-gather.2.cloned.1.call-done = bf16[4096,3,256]{2,0,1:T(8,128)(2,1)} async-done(((bf16[64,3,256]{2,0,1:T(8,128)(2,1)}), bf16[4096,3,256]{2,0,1:T(8,128)(2,1)}) %all-gather.2.cloned.1.call-update) | async-done | bytes 6291472 | tf_op jit(solution)/shard_map/all_gather | solution.py:89
  100.6 8.7 %copy.47 = bf16[4096,3,256]{0,2,1:T(8,128)(2,1)} copy(bf16[4096,3,256]{2,0,1:T(8,128)(2,1)} %all-gather.2.cloned.1.call-done) | data formatting | bytes 12582912 | tf_op jit(solution)/shard_map/all_gather | solution.py:89
  109.3 5.0 %convolution_convert_fusion.1 = bf16[128,768]{1,0:T(8,128)(2,1)S(1)} fusion(bf16[4096,768]{0,1:T(8,128)(2,1)} %bitcast.138, bf16[128,4096]{1,0:T(8,128)(2,1)S(1)} %copy-done, f32[4096]{0:T(1024)S(1)} %copy-done.6, f32[128]{0:T(128)S(1)} %get-tuple-element.16), kind=kOutput, calls=%fused_computation.16 | convolution fusion | flops 807501824 | bytes 7553536 | tf_op jit(solution)/shard_map/dot_general | solution.py:98
  114.9 2.7 collective-permute-start
  117.6 2.3 fusion.149
  120.5 0.7 copy-done.4
  121.2 0.8 maximum_bitcast_fusion
  122.0 2.0 copy.51
  124.0 8.8 %all-to-all-start.1 = ((f32[3,256,128]{2,0,1:T(4,128)}), f32[3,256,128]{2,0,1:T(4,128)}, u32[]{:S(2)}, u32[]{:S(2)}) async-start(f32[3,256,128]{2,0,1:T(4,128)} %copy.51), calls=%async_computation.1 | async-start | bytes 1048576 | tf_op jit(solution)/shard_map/all_to_all | solution.py:18
  133.0 0.9 fusion.85
  133.9 1.6 copy.54
  135.5 0.9 fusion.84
  136.4 1.6 copy.55
  137.9 12.1 %all-to-all-done.1 = f32[3,256,128]{2,0,1:T(4,128)} async-done(((f32[3,256,128]{2,0,1:T(4,128)}), f32[3,256,128]{2,0,1:T(4,128)}, u32[]{:S(2)}, u32[]{:S(2)}) %all-to-all-start.1) | async-done | bytes 393248 | tf_op jit(solution)/shard_map/all_to_all | solution.py:18
  150.0 2.6 convolution_bitcast_fusion.1
  152.6 2.5 fusion
  155.1 1.6 fusion.31
  156.7 1.6 fusion.32
  158.3 1.6 convolution_add_fusion.1
  160.0 1.6 convolution_subtract_fusion.1
  161.8 1.1 fusion.13
  162.9 1.3 fusion.12
  164.3 1.1 convolution_subtract_fusion
  165.4 1.1 convolution_add_fusion
  166.5 1.2 fusion.8
  167.6 1.9 fusion.2
  169.6 9.6 %copy.86 = f32[3,4,64,128]{1,0,3,2:T(4,128)} copy(f32[3,4,64,128]{3,2,1,0:T(8,128)} %fusion.2) | data formatting | bytes 786432 | tf_op jit(solution)/shard_map/div | solution.py:75
  179.2 16.7 %reshape.122 = f32[64,1,1536]{2,1,0:T(1,128)} reshape(f32[8192,3,4]{2,1,0:T(4,128)} %bitcast.134) | data formatting | bytes 786432
  195.9 20.9 %all_to_all.38 = f32[64,1,1536]{2,1,0:T(1,128)} all-to-all(f32[64,1,1536]{2,1,0:T(1,128)} %reshape.122), channel_id=1, replica_groups=mesh['seq'=64,'ch'=4] {'seq'}, dimensions={0} | all-to-all | bytes 786432 | tf_op jit(solution)/shard_map/all_to_all | solution.py:22
  217.3 3.3 reduce
  220.7 12.4 %reshape.123 = f32[8192,3,4]{2,1,0:T(4,128)} reshape(f32[64,1536]{1,0:T(8,128)} %reduce) | data formatting | bytes 786432
  233.0 10.1 %copy.87 = f32[3,4,64,128]{3,2,1,0:T(8,128)} copy(f32[3,4,64,128]{1,0,3,2:T(4,128)} %bitcast.135) | data formatting | bytes 786432 | tf_op jit(solution)/shard_map/all_to_all | solution.py:22
  243.1 2.0 copy.68
  245.1 1.9 copy.69
  247.0 2.7 convolution_convert_fusion
  249.8 1.1 fusion.39
  250.9 2.6 collective-permute-start.1
  253.5 2.4 collective-permute-done.1
  255.9 6.3 %convolution_bitcast_fusion = f32[128,4096]{1,0:T(8,128)} fusion(bf16[4096,3,256]{2,0,1:T(8,128)(2,1)} %all-gather.2.cloned.1.call-done, f32[130,3,256]{2,0,1:T(8,128)S(1)} %pad_maximum_fusion.6, f32[3,256]{1,0:T(4,128)S(1)} %get-tuple-element.17, f32[3,256]{1,0:T(4,128)S(1)} %get-tuple-element.18, f32[3,256]{1,0:T(4,128)S(1)} %bitcast.146, ...), kind=kOutput, calls=%fused_computation | convolution fusion | flops 806092800 | bytes 9580544 | tf_op jit(solution)/shard_map/dot_general | solution.py:149
  262.5 1.6 fusion.33
  264.1 7.7 %reduce-scatter.2.cloned.1.call-done = bf16[128,1024]{1,0:T(8,128)(2,1)} async-done(((bf16[128,4096]{1,0:T(8,128)(2,1)}), bf16[128,1024]{1,0:T(8,128)(2,1)}) %reduce-scatter.2.cloned.1.call-update) | async-done | bytes 262160 | tf_op jit(solution)/shard_map/reduce_scatter | solution.py:132
  271.7 1.7 add_convert_fusion
  273.4 65.5 %all-reduce.2.cloned.1.call-done = f32[128,4096]{1,0:T(8,128)} async-done(((f32[128,4096]{1,0:T(8,128)}), f32[128,4096]{1,0:T(8,128)}) %all-reduce.2.cloned.1.call-update) | async-done | bytes 2097168 | tf_op jit(solution)/shard_map/psum | solution.py:150
  339.0 2.1 multiply_reduce_fusion
  341.2 3.1 subtract_convert_fusion
  (53 shorter events, 3.5 us)
Async XLA Ops:
  7.2 93.4 %all-gather.2.cloned.1.call-start = ((), (), s32[]{:S(2)}) async-start(), calls=%async_computation.4 | async-start | bytes 6389760 | tf_op jit(solution)/shard_map/all_gather | solution.py:89
  10.3 13.1 %copy-start.8 = (f32[3,3,256]{2,1,0:T(4,128)S(1)}, f32[3,3,256]{2,1,0:T(4,128)}, u32[]{:S(2)}) copy-start(f32[3,3,256]{2,1,0:T(4,128)} %param.11) | copy-start | bytes 27652
  10.3 13.2 %copy-start = (bf16[128,4096]{1,0:T(8,128)(2,1)S(1)}, bf16[128,4096]{1,0:T(8,128)(2,1)}, u32[]{:S(2)}) copy-start(bf16[128,4096]{1,0:T(8,128)(2,1)} %param.8) | copy-start | bytes 3145732
  10.3 107.3 %all-to-all-start = ((bf16[64,256,64]{1,2,0:T(8,128)(2,1)}), bf16[64,256,64]{1,2,0:T(8,128)(2,1)S(1)}, u32[]{:S(2)}, u32[]{:S(2)}) async-start(bf16[64,256,64]{1,2,0:T(8,128)(2,1)} %stack.21), calls=%async_computation | async-start | bytes 4194304 | tf_op jit(solution)/shard_map/all_to_all | solution.py:91
  24.3 85.0 %copy-start.11 = (f32[128]{0:T(128)}, f32[128]{0:T(128)S(1)}, u32[]{:S(2)}) copy-start(f32[128]{0:T(128)S(1)} %get-tuple-element.16) | copy-start | bytes 1540
  24.3 85.0 %copy-start.6 = (f32[4096]{0:T(1024)S(1)}, f32[4096]{0:T(1024)}, u32[]{:S(2)}) copy-start(f32[4096]{0:T(1024)} %param.9) | copy-start | bytes 49156
  114.9 5.4 %collective-permute-start = (bf16[2,3,256]{2,0,1:T(2,128)(2,1)}, bf16[2,3,256]{2,0,1:T(2,128)(2,1)S(1)}, u32[]{:S(2)}, u32[]{:S(2)}) collective-permute-start(bf16[2,3,256]{2,0,1:T(2,128)(2,1)} %bitcast.1), channel_id=1, source_target_pairs={{0,4},{4,8},{8,12},{12,16},{16,20},{20,24},{24,28},{28,32},{32,36}... | collective-permute-start | bytes 9224 | tf_op jit(solution)/shard_map/ppermute | solution.py:14
  120.3 0.9 copy-start.4
  120.3 1.0 copy-start.5
  124.0 26.0 %all-to-all-start.1 = ((f32[3,256,128]{2,0,1:T(4,128)}), f32[3,256,128]{2,0,1:T(4,128)}, u32[]{:S(2)}, u32[]{:S(2)}) async-start(f32[3,256,128]{2,0,1:T(4,128)} %copy.51), calls=%async_computation.1 | async-start | bytes 1048576 | tf_op jit(solution)/shard_map/all_to_all | solution.py:18
  132.8 138.9 %reduce-scatter.2.cloned.1.call-start = ((), (), s32[]{:S(2)}) async-start(), calls=%async_computation.5 | async-start | bytes 1310720 | tf_op jit(solution)/shard_map/reduce_scatter | solution.py:132
  150.0 5.1 %copy-start.2 = (f32[128,128]{0,1:T(8,128)S(1)}, f32[128,128]{0,1:T(8,128)}, u32[]{:S(2)}) copy-start(f32[128,128]{0,1:T(8,128)} %copy.54) | copy-start | bytes 196612
  150.0 5.1 %copy-start.3 = (f32[128,128]{0,1:T(8,128)S(1)}, f32[128,128]{0,1:T(8,128)}, u32[]{:S(2)}) copy-start(f32[128,128]{0,1:T(8,128)} %copy.55) | copy-start | bytes 196612
  233.0 14.0 %copy-start.9 = (f32[256]{0:T(256)S(1)}, f32[256]{0:T(256)}, u32[]{:S(2)}) copy-start(f32[256]{0:T(256)} %param.13) | copy-start | bytes 3076
  249.7 89.3 %all-reduce.2.cloned.1.call-start = ((), (), s32[]{:S(2)}) async-start(), calls=%async_computation.6 | async-start | bytes 4194304 | tf_op jit(solution)/shard_map/psum | solution.py:150
  250.9 4.9 %collective-permute-start.1 = (f32[2,3,256]{2,0,1:T(2,128)S(1)}, f32[2,3,256]{2,0,1:T(2,128)S(1)}, u32[]{:S(2)}, u32[]{:S(2)}) collective-permute-start(f32[2,3,256]{2,0,1:T(2,128)S(1)} %slice.110), channel_id=1, source_target_pairs={{4,0},{8,4},{12,8},{16,12},{20,16},{24,20},{28,24},{32,28},{36,32}... | collective-permute-start | bytes 18440 | tf_op jit(solution)/shard_map/ppermute | solution.py:14
  262.3 76.7 %copy-start.7 = (f32[4096]{0:T(1024)S(1)}, f32[4096]{0:T(1024)}, u32[]{:S(2)}) copy-start(f32[4096]{0:T(1024)} %param.9) | copy-start | bytes 49156
  264.1 77.0 %copy-start.10 = (f32[128]{0:T(128)S(1)}, f32[128]{0:T(128)}, u32[]{:S(2)}) copy-start(f32[128]{0:T(128)} %get-tuple-element.15) | copy-start | bytes 1540
  264.1 77.0 %copy-start.12 = (f32[128]{0:T(128)S(1)}, f32[128]{0:T(128)}, u32[]{:S(2)}) copy-start(f32[128]{0:T(128)} %copy-done.11) | copy-start | bytes 1540
  339.0 2.2 copy-start.1
Sparse Core Ops, SparseCore 0:
  10.8 89.7 all-gather.1
  249.8 21.8 reduce-scatter.1
  274.1 64.8 all-reduce.1
